TPU v7x, 32 devices: a whole 2x2x4 slice. The times are simulated.
32 devices in a mesh: dp: 4 (over z), fsdp: 2 (over x), rows: 4 (over y, core).
Axes of the slice: x: 2, y: 2, z: 4, core: 2. Of those that a mesh axis runs over, the one named last changes fastest.
Arguments:
- feature_maps: bfloat16 [8, 16, 32, 1536], P(('dp', 'fsdp'), 'rows'), may hold values from -30 to 30
- dw_kernel: float32 [7, 7, 1536], replicated, may hold values from -0.875 to 0.875
- norm_gain: float32 [1536], replicated, may hold values from 0.5 to 1.5
- w_up: bfloat16 [1536, 6144], P(('dp', 'rows'), 'fsdp'), may hold values from -0.15625 to 0.15625
- w_down: bfloat16 [6144, 1536], P('fsdp', ('dp', 'rows')), may hold values from -0.078125 to 0.078125
- layer_scale: float32 [1536], replicated, may hold values from 0.3 to 1.5
- d_out: bfloat16 [8, 16, 32, 1536], P(('dp', 'fsdp'), 'rows'), may hold values from -20 to 20
Outputs:
- result: bfloat16 [8, 16, 32, 1536], P(('dp', 'fsdp'), 'rows')
- grad_x: bfloat16 [8, 16, 32, 1536], P(('dp', 'fsdp'), 'rows')
- grad_up: float32 [1536, 6144], P(('dp', 'rows'), 'fsdp')
- grad_down: float32 [6144, 1536], P('fsdp', ('dp', 'rows'))
- grad_kernel: float32 [7, 7, 1536], replicated
- grad_gain: float32 [1536], replicated
- grad_scale: float32 [1536], replicated
All inputs are finite; a program needn't handle non-finite values.
Results may differ from a plain program's by a relative error of at most 0.0075.
Values may be sent and summed in bfloat16 or wider, within the bound.
No kernel may reach another device: no remote copies, remote signals or barrier semaphores. Data moves between devices by JAX's collectives and lax.ppermute only.
A program may use at most 128 MiB of HBM per device.

v0:
```python
import math
import jax
import jax.numpy as jnp
from jax import lax
from jax.sharding import PartitionSpec as P

KS = 7
norm_eps = 1e-06
inv_root_two = 1.0 / math.sqrt(2.0)
inv_root_two_pi = 1.0 / math.sqrt(2.0 * math.pi)
contract_rows = (((0,), (0,)), ((), ()))
contract_cols = (((1,), (1,)), ((), ()))


def padded_2(x, sides, width):
    for axis, dim in sides:
        devices, length = (lax.axis_size(axis), x.shape[dim])
        up = [(i, (i + 1) % devices) for i in range(devices - 1)]
        down = [(j, i) for i, j in up]
        last = lax.slice_in_dim(x, length - width, length, axis=dim)
        leading = lax.slice_in_dim(x, 0, width, axis=dim)
        before = lax.ppermute(last, axis, up)
        after = lax.ppermute(leading, axis, down)
        x = jnp.concatenate([before, x, after], axis=dim)
    return x


def gelu_exact(values):
    return 0.5 * values * (1.0 + jax.scipy.special.erf(values * inv_root_two))


def gelu_slope(values):
    cdf_part = 0.5 * (1.0 + jax.scipy.special.erf(values * inv_root_two))
    return cdf_part + values * jnp.exp(-0.5 * values * values) * inv_root_two_pi


def reduce_down(down_part):
    return lax.psum_scatter(down_part, ("dp", "rows"), scatter_dimension=1, tiled=True)


def body(feature_maps, dw_kernel, norm_gain, w_up, w_down, layer_scale, d_out):
    scenes, strip, across, width = feature_maps.shape
    cells = scenes * strip * across
    rimmed = padded_2(feature_maps, (("rows", 1),), 3)
    padded = jnp.pad(rimmed.astype(jnp.float32), ((0, 0), (0, 0), (3, 3), (0, 0)))
    filtered = jnp.zeros(feature_maps.shape, jnp.float32)
    for row_off in range(KS):
        for col_off in range(KS):
            filtered = (
                filtered
                + padded[:, row_off : row_off + strip, col_off : col_off + across, :]
                * dw_kernel[row_off, col_off]
            )
    flat = filtered.reshape(cells, width)
    average = jnp.mean(flat, axis=-1, keepdims=True)
    center = flat - average
    variance = jnp.mean(center * center, axis=-1, keepdims=True)
    rstd = lax.rsqrt(variance + norm_eps)
    normed = center * rstd
    scaled = (normed * norm_gain).astype(jnp.bfloat16)
    gathered = lax.all_gather(scaled, "fsdp", axis=0, tiled=True)
    up_full = lax.all_gather(w_up, ("dp", "rows"), axis=0, tiled=True)
    down_full = lax.all_gather(w_down, ("dp", "rows"), axis=1, tiled=True)
    hidden = jnp.dot(gathered, up_full, preferred_element_type=jnp.float32)
    active = gelu_exact(hidden).astype(jnp.bfloat16)
    mlp_terms = jnp.dot(active, down_full, preferred_element_type=jnp.float32)
    branch = lax.psum_scatter(
        mlp_terms.astype(jnp.bfloat16), "fsdp", scatter_dimension=0, tiled=True
    ).astype(jnp.float32)
    resid = feature_maps.reshape(cells, width).astype(jnp.float32)
    result = (resid + layer_scale * branch).astype(jnp.bfloat16).reshape(feature_maps.shape)
    cotan = d_out.reshape(cells, width).astype(jnp.float32)
    scale_part = jnp.sum(cotan * branch, axis=0)
    back = (cotan * layer_scale).astype(jnp.bfloat16)
    back_all = lax.all_gather(back, "fsdp", axis=0, tiled=True)
    down_part = lax.dot_general(active, back_all, contract_rows, preferred_element_type=jnp.float32)
    slope_in = lax.dot_general(
        back_all, down_full, contract_cols, preferred_element_type=jnp.float32
    )
    hidden_grad = (slope_in * gelu_slope(hidden)).astype(jnp.bfloat16)
    up_part = lax.dot_general(
        gathered, hidden_grad, contract_rows, preferred_element_type=jnp.float32
    )
    norm_terms = lax.dot_general(
        hidden_grad, up_full, contract_cols, preferred_element_type=jnp.float32
    )
    norm_grad = lax.psum_scatter(norm_terms, "fsdp", scatter_dimension=0, tiled=True)
    grad_up = lax.psum_scatter(up_part, ("dp", "rows"), scatter_dimension=0, tiled=True)
    grad_down = reduce_down(down_part)
    gain_part = jnp.sum(norm_grad * normed, axis=0)
    scaled_grad = norm_grad * norm_gain
    conv_grad = rstd * (
        scaled_grad
        - jnp.mean(scaled_grad, axis=-1, keepdims=True)
        - normed * jnp.mean(scaled_grad * normed, axis=-1, keepdims=True)
    )
    conv_grad = conv_grad.reshape(feature_maps.shape)
    grad_rim = padded_2(conv_grad.astype(jnp.bfloat16), (("rows", 1),), 3).astype(conv_grad.dtype)
    grad_pad = jnp.pad(grad_rim, ((0, 0), (0, 0), (3, 3), (0, 0)))
    kernel_rows = []
    back_conv = jnp.zeros(feature_maps.shape, jnp.float32)
    for row_off in range(KS):
        for col_off in range(KS):
            window = padded[:, row_off : row_off + strip, col_off : col_off + across, :]
            kernel_rows.append(jnp.sum(window * conv_grad, axis=(0, 1, 2)))
            back_conv = (
                back_conv
                + grad_pad[
                    :, 6 - row_off : 6 - row_off + strip, 6 - col_off : 6 - col_off + across, :
                ]
                * dw_kernel[row_off, col_off]
            )
    kernel_part = jnp.stack(kernel_rows).reshape(KS, KS, width)
    grad_x = (d_out.astype(jnp.float32) + back_conv).astype(jnp.bfloat16)
    grad_kernel, grad_gain, grad_scale = lax.psum(
        (kernel_part, gain_part, scale_part), ("dp", "fsdp", "rows")
    )
    return (result, grad_x, grad_up, grad_down, grad_kernel, grad_gain, grad_scale)


def solution(mesh):
    return jax.shard_map(
        body,
        mesh=mesh,
        in_specs=(
            P(("dp", "fsdp"), "rows", None, None),
            P(),
            P(),
            P(("dp", "rows"), "fsdp"),
            P("fsdp", ("dp", "rows")),
            P(),
            P(("dp", "fsdp"), "rows", None, None),
        ),
        out_specs=(
            P(("dp", "fsdp"), "rows", None, None),
            P(("dp", "fsdp"), "rows", None, None),
            P(("dp", "rows"), "fsdp"),
            P("fsdp", ("dp", "rows")),
            P(),
            P(),
            P(),
        ),
        check_vma=False,
    )
```

profile of v0, /device:TPU:0, one launch (start us, length us, event | category | flops | bytes accessed | tf_op | source)
XLA Modules:
  0.0 797.9 jit_solution(10668589192870983978)
XLA Ops:
  8.7 1.1 fusion.105
  9.8 2.4 collective-permute-start
  12.2 1.3 collective-permute-start.1
  13.5 1.3 slice_reduce_fusion.46
  16.4 1.4 collective-permute-done.1
  18.0 9.5 %fusion.103 = (f32[4,32]{1,0:T(4,128)S(1)}, f32[1,4,32,1536]{3,2,1,0:T(8,128)S(1)}) fusion(f32[1536]{0:T(1024)S(1)} %get-tuple-element.106, f32[1536]{0:T(1024)S(1)} %get-tuple-element.107, f32[1536]{0:T(1024)S(1)} %get-tuple-element.60, f32[1536]{0:T(1024)S(1)} %get-tuple-element.61, f32[1,10,32,1536]{3,2,1,0:T(8,128)S(1)} %maximum_convert_fusion, ...), kind=kLoop, calls=%fused_computation.314 | loop fusion | flops 19267456 | bytes 8641024 | tf_op jit(solution)/shard_map/reduce_sum | solution.py:55
  30.1 8.6 %all_gather.12 = bf16[256,1536]{1,0:T(8,128)(2,1)} all-gather(bf16[128,1536]{1,0:T(8,128)(2,1)S(1)} %multiply_convert_fusion.1), channel_id=1, replica_groups=mesh['dp'=4,'fsdp'=2,'rows'=4] {'fsdp'}, dimensions={0}, use_global_device_ids=true | all-gather | bytes 1179648 | tf_op jit(solution)/shard_map/all_gather | solution.py:61
  38.7 55.8 %all-gather.3.cloned.1.call-done = bf16[1536,3072]{1,0:T(8,128)(2,1)} async-done(((bf16[96,3072]{1,0:T(8,128)(2,1)}), bf16[1536,3072]{1,0:T(8,128)(2,1)}) %all-gather.3.cloned.1.call-update) | async-done | bytes 9437200 | tf_op jit(solution)/shard_map/all_gather | solution.py:62
  94.5 8.2 %fusion.106 = f32[256,3072]{1,0:T(8,128)} fusion(bf16[256,1536]{1,0:T(8,128)(2,1)} %all_gather.12, bf16[1536,3072]{1,0:T(8,128)(2,1)} %all-gather.3.cloned.1.call-done), kind=kOutput, calls=%fused_computation.317 | convolution fusion | flops 2415919104 | bytes 13369344 | tf_op jit(solution)/shard_map/dot_general | solution.py:64
  102.7 73.7 %all-gather.5.cloned.1.call-done = bf16[3072,1536]{0,1:T(8,128)(2,1)} async-done(((bf16[3072,96]{0,1:T(8,128)(2,1)}), bf16[3072,1536]{0,1:T(8,128)(2,1)}) %all-gather.5.cloned.1.call-update) | async-done | bytes 9437200 | tf_op jit(solution)/shard_map/all_gather | solution.py:63
  176.4 8.2 %convolution_convert_fusion = bf16[256,1536]{1,0:T(8,128)(2,1)} fusion(bf16[3072,1536]{0,1:T(8,128)(2,1)} %all-gather.5.cloned.1.call-done, f32[256,3072]{1,0:T(8,128)} %fusion.106), kind=kOutput, calls=%fused_computation.93 | convolution fusion | flops 2420244480 | bytes 13369344 | tf_op jit(solution)/shard_map/dot_general | solution.py:66
  184.6 15.7 %reduce-scatter.5.cloned.1.call-done = bf16[128,1536]{1,0:T(8,128)(2,1)} async-done(((bf16[256,1536]{1,0:T(8,128)(2,1)}), bf16[128,1536]{1,0:T(8,128)(2,1)}) %reduce-scatter.5.cloned.1.call-update) | async-done | bytes 393232 | tf_op jit(solution)/shard_map/reduce_scatter | solution.py:67
  200.3 2.7 fusion.7
  203.0 11.8 %all_gather.15 = bf16[256,1536]{1,0:T(8,128)(2,1)S(1)} all-gather(bf16[128,1536]{1,0:T(8,128)(2,1)S(1)} %get-tuple-element.114), channel_id=1, replica_groups=mesh['dp'=4,'fsdp'=2,'rows'=4] {'fsdp'}, dimensions={0}, use_global_device_ids=true | all-gather | bytes 1179648 | tf_op jit(solution)/shard_map/all_gather | solution.py:75
  215.7 5.5 fusion
  221.3 1.2 copy-done.7
  222.5 3.8 fusion.107
  226.4 26.2 %reduce-scatter.7.cloned.1.call-done = f32[128,1536]{1,0:T(8,128)} async-done(((f32[256,1536]{1,0:T(8,128)}), f32[128,1536]{1,0:T(8,128)}) %reduce-scatter.7.cloned.1.call-update) | async-done | bytes 786448 | tf_op jit(solution)/shard_map/reduce_scatter | solution.py:87
  252.6 2.0 multiply_reduce_fusion
  254.6 3.6 multiply_reduce_fusion.2
  258.2 1.2 multiply_reduce_fusion.3
  259.4 2.0 multiply_reduce_fusion.1
  263.5 11.1 %fusion.102 = f32[3072,1536]{0,1:T(8,128)} fusion(bf16[256,1536]{1,0:T(8,128)(2,1)S(1)} %copy-done.3, f32[256,3072]{1,0:T(8,128)} %fusion.106), kind=kOutput, calls=%fused_computation.313 | convolution fusion | flops 2419851264 | bytes 22806528 | tf_op jit(solution)/shard_map/dot_general | solution.py:76
  276.2 7.9 fusion.108
  284.7 1.9 collective-permute-start.2
  286.5 1.3 collective-permute-start.3
  287.9 42.3 %all-reduce.2 = (f32[1536]{0:T(1024)}, f32[1536]{0:T(1024)}) all-reduce(f32[1536]{0:T(1024)} %get-tuple-element.56, f32[1536]{0:T(1024)} %get-tuple-element.113), channel_id=1, replica_groups=mesh['dp'=4,'fsdp'=2,'rows'=4] {'dp','fsdp','rows'}, use_global_device_ids=true, to_apply=%region_59.60 | all-reduce | flops 3072 | bytes 24576 | tf_op jit(solution)/shard_map/psum | solution.py:115
  330.7 7.5 fusion.95
  338.3 51.2 %all-reduce.5.cloned.1.call-done = f32[7,7,1536]{2,1,0:T(8,128)} async-done(((f32[7,7,1536]{2,1,0:T(8,128)}), f32[7,7,1536]{2,1,0:T(8,128)}) %all-reduce.5.cloned.1.call-update) | async-done | bytes 301072 | tf_op jit(solution)/shard_map/psum | solution.py:115
  389.4 200.8 %reduce-scatter.11.cloned.1.call-done = f32[3072,96]{0,1:T(8,128)} async-done(((f32[3072,1536]{0,1:T(8,128)}), f32[3072,96]{0,1:T(8,128)}) %reduce-scatter.11.cloned.1.call-update) | async-done | bytes 1179664 | tf_op jit(solution)/shard_map/reduce_scatter | solution.py:38
  590.2 199.1 %reduce-scatter.9.cloned.1.call-done = f32[96,3072]{1,0:T(8,128)} async-done(((f32[1536,3072]{1,0:T(8,128)}), f32[96,3072]{1,0:T(8,128)}) %reduce-scatter.9.cloned.1.call-update) | async-done | bytes 1179664 | tf_op jit(solution)/shard_map/reduce_scatter | solution.py:88
  789.3 1.7 copy.15
  (270 shorter events, 10.1 us)
Async XLA Ops:
  7.2 87.3 %all-gather.3.cloned.1.call-start = ((), (), s32[]{:S(2)}) async-start(), calls=%async_computation.4 | async-start | bytes 10027008 | tf_op jit(solution)/shard_map/all_gather | solution.py:62
  7.9 168.5 %all-gather.5.cloned.1.call-start = ((), (), s32[]{:S(2)}) async-start(), calls=%async_computation.5 | async-start | bytes 10027008 | tf_op jit(solution)/shard_map/all_gather | solution.py:63
  8.7 191.6 %reduce-scatter.5.cloned.1.call-start = ((), (), s32[]{:S(2)}) async-start(), calls=%async_computation.6 | async-start | bytes 1179648 | tf_op jit(solution)/shard_map/reduce_scatter | solution.py:67
  9.8 6.6 collective-permute-start
  12.2 5.6 collective-permute-start.1
  102.7 97.6 %copy-start.5 = (bf16[1,4,32,1536]{3,2,1,0:T(8,128)(2,1)S(1)}, bf16[1,4,32,1536]{3,2,1,0:T(8,128)(2,1)}, u32[]{:S(2)}) copy-start(bf16[1,4,32,1536]{3,2,1,0:T(8,128)(2,1)} %param.13) | copy-start | bytes 1179652
  184.6 68.0 %reduce-scatter.7.cloned.1.call-start = ((), (), s32[]{:S(2)}) async-start(), calls=%async_computation.7 | async-start | bytes 2359296 | tf_op jit(solution)/shard_map/reduce_scatter | solution.py:87
  226.3 163.1 %all-reduce.5.cloned.1.call-start = ((), (), s32[]{:S(2)}) async-start(), calls=%async_computation.10 | async-start | bytes 688128 | tf_op jit(solution)/shard_map/psum | solution.py:115
  263.4 326.7 %reduce-scatter.11.cloned.1.call-start = ((), (), s32[]{:S(2)}) async-start(), calls=%async_computation.9 | async-start | bytes 20054016 | tf_op jit(solution)/shard_map/reduce_scatter | solution.py:38
  274.6 514.7 %reduce-scatter.9.cloned.1.call-start = ((), (), s32[]{:S(2)}) async-start(), calls=%async_computation.8 | async-start | bytes 20054016 | tf_op jit(solution)/shard_map/reduce_scatter | solution.py:88
  284.2 46.1 %copy-start.6 = (bf16[1,4,32,1536]{3,2,1,0:T(8,128)(2,1)S(1)}, bf16[1,4,32,1536]{3,2,1,0:T(8,128)(2,1)}, u32[]{:S(2)}) copy-start(bf16[1,4,32,1536]{3,2,1,0:T(8,128)(2,1)} %param.13) | copy-start | bytes 1179652
  284.2 46.1 %copy-start.12 = (f32[1536]{0:T(1024)S(1)}, f32[1536]{0:T(1024)}, u32[]{:S(2)}) copy-start(f32[1536]{0:T(1024)} %copy-done.11) | copy-start | bytes 18436
  284.2 46.1 %copy-start.14 = (f32[1536]{0:T(1024)S(1)}, f32[1536]{0:T(1024)}, u32[]{:S(2)}) copy-start(f32[1536]{0:T(1024)} %copy-done.13) | copy-start | bytes 18436
  284.2 46.1 %copy-start.16 = (f32[1536]{0:T(1024)S(1)}, f32[1536]{0:T(1024)}, u32[]{:S(2)}) copy-start(f32[1536]{0:T(1024)} %copy-done.15) | copy-start | bytes 18436
  284.2 46.1 %copy-start.18 = (f32[1536]{0:T(1024)S(1)}, f32[1536]{0:T(1024)}, u32[]{:S(2)}) copy-start(f32[1536]{0:T(1024)} %copy-done.17) | copy-start | bytes 18436
  284.3 46.1 %copy-start.20 = (f32[1536]{0:T(1024)S(1)}, f32[1536]{0:T(1024)}, u32[]{:S(2)}) copy-start(f32[1536]{0:T(1024)} %copy-done.19) | copy-start | bytes 18436
  284.3 46.1 %copy-start.22 = (f32[1536]{0:T(1024)S(1)}, f32[1536]{0:T(1024)}, u32[]{:S(2)}) copy-start(f32[1536]{0:T(1024)} %copy-done.21) | copy-start | bytes 18436
  284.3 46.1 %copy-start.24 = (f32[1536]{0:T(1024)S(1)}, f32[1536]{0:T(1024)}, u32[]{:S(2)}) copy-start(f32[1536]{0:T(1024)} %copy-done.23) | copy-start | bytes 18436
  284.3 46.1 %copy-start.26 = (f32[1536]{0:T(1024)S(1)}, f32[1536]{0:T(1024)}, u32[]{:S(2)}) copy-start(f32[1536]{0:T(1024)} %copy-done.25) | copy-start | bytes 18436
  284.3 46.1 %copy-start.28 = (f32[1536]{0:T(1024)S(1)}, f32[1536]{0:T(1024)}, u32[]{:S(2)}) copy-start(f32[1536]{0:T(1024)} %copy-done.27) | copy-start | bytes 18436
  284.3 46.1 %copy-start.30 = (f32[1536]{0:T(1024)S(1)}, f32[1536]{0:T(1024)}, u32[]{:S(2)}) copy-start(f32[1536]{0:T(1024)} %copy-done.29) | copy-start | bytes 18436
  284.3 46.1 %copy-start.32 = (f32[1536]{0:T(1024)S(1)}, f32[1536]{0:T(1024)}, u32[]{:S(2)}) copy-start(f32[1536]{0:T(1024)} %copy-done.31) | copy-start | bytes 18436
  284.3 46.1 %copy-start.34 = (f32[1536]{0:T(1024)S(1)}, f32[1536]{0:T(1024)}, u32[]{:S(2)}) copy-start(f32[1536]{0:T(1024)} %copy-done.33) | copy-start | bytes 18436
  284.3 46.1 %copy-start.36 = (f32[1536]{0:T(1024)S(1)}, f32[1536]{0:T(1024)}, u32[]{:S(2)}) copy-start(f32[1536]{0:T(1024)} %copy-done.35) | copy-start | bytes 18436
  284.3 46.1 %copy-start.38 = (f32[1536]{0:T(1024)S(1)}, f32[1536]{0:T(1024)}, u32[]{:S(2)}) copy-start(f32[1536]{0:T(1024)} %copy-done.37) | copy-start | bytes 18436
  284.4 46.1 %copy-start.40 = (f32[1536]{0:T(1024)S(1)}, f32[1536]{0:T(1024)}, u32[]{:S(2)}) copy-start(f32[1536]{0:T(1024)} %copy-done.39) | copy-start | bytes 18436
  284.4 46.1 %copy-start.42 = (f32[1536]{0:T(1024)S(1)}, f32[1536]{0:T(1024)}, u32[]{:S(2)}) copy-start(f32[1536]{0:T(1024)} %copy-done.41) | copy-start | bytes 18436
  284.4 46.1 %copy-start.44 = (f32[1536]{0:T(1024)S(1)}, f32[1536]{0:T(1024)}, u32[]{:S(2)}) copy-start(f32[1536]{0:T(1024)} %copy-done.43) | copy-start | bytes 18436
  284.4 46.1 %copy-start.46 = (f32[1536]{0:T(1024)S(1)}, f32[1536]{0:T(1024)}, u32[]{:S(2)}) copy-start(f32[1536]{0:T(1024)} %copy-done.45) | copy-start | bytes 18436
  284.4 46.1 %copy-start.48 = (f32[1536]{0:T(1024)S(1)}, f32[1536]{0:T(1024)}, u32[]{:S(2)}) copy-start(f32[1536]{0:T(1024)} %copy-done.47) | copy-start | bytes 18436
  284.7 45.5 %collective-permute-start.2 = (bf16[1,3,32,1536]{3,2,1,0:T(8,128)(2,1)S(1)}, bf16[1,3,32,1536]{3,2,1,0:T(8,128)(2,1)S(1)}, u32[]{:S(2)}, u32[]{:S(2)}) collective-permute-start(bf16[1,3,32,1536]{3,2,1,0:T(8,128)(2,1)S(1)} %get-tuple-element.116), channel_id=1, source_target_pairs={{0,1},{1,2},{2,3},{4,5},{5,6},{6,7},{8,9},{9,10},{10,11},{12,13},{... | collective-permute-start | bytes 884744 | tf_op jit(solution)/shard_map/ppermute | solution.py:22
  286.5 43.6 %collective-permute-start.3 = (bf16[1,3,32,1536]{3,2,1,0:T(8,128)(2,1)S(1)}, bf16[1,3,32,1536]{3,2,1,0:T(8,128)(2,1)S(1)}, u32[]{:S(2)}, u32[]{:S(2)}) collective-permute-start(bf16[1,3,32,1536]{3,2,1,0:T(8,128)(2,1)S(1)} %get-tuple-element.117), channel_id=1, source_target_pairs={{1,0},{2,1},{3,2},{5,4},{6,5},{7,6},{9,8},{10,9},{11,10},{13,12},{... | collective-permute-start | bytes 884744 | tf_op jit(solution)/shard_map/ppermute | solution.py:23
  (73 other events, 1542.2 us)
Sparse Core Ops, SparseCore 0:
  10.3 84.1 all-gather.2
  96.8 79.5 all-gather.4
  184.7 15.5 reduce-scatter.4
  226.4 26.0 reduce-scatter.6
  263.6 125.8 all-reduce.4
  394.5 195.6 reduce-scatter.10
  595.4 193.8 reduce-scatter.8
where the time goes:
time: 799 us; the launch traced here: 798 us
  waiting for transfers between devices  625 us (78%)
  blocking collectives  62.7 us (8%)
  matrix products  44.7 us (6%)
  other arithmetic  30 us (4%)
  between operations  16 us (2%)
  local copies, waits for them, and re-layouts  12.1 us (2%)
    reduce_scatter x1, waiting for transfers between devices, reduce_down(): lax.psum_scatter(down_part, ('dp', 'rows'), scatter_dimension=1, tiled=True)  201 us
    reduce_scatter x1, waiting for transfers between devices, body(): lax.psum_scatter(up_part, ('dp', 'rows'), scatter_dimension=0, tiled=True)  199 us
    all_gather x1, waiting for transfers between devices, body(): down_full = lax.all_gather(w_down, ('dp', 'rows'), axis=1, tiled=True)  73.7 us
    all_gather x1, waiting for transfers between devices, body(): up_full = lax.all_gather(w_up, ('dp', 'rows'), axis=0, tiled=True)  55.8 us
    psum x1, waiting for transfers between devices, body(): lax.psum((kernel_part, gain_part, scale_part), ('dp', 'fsdp', 'rows'))  51.2 us
    psum x1, blocking collectives, body(): lax.psum((kernel_part, gain_part, scale_part), ('dp', 'fsdp', 'rows'))  42.3 us
    reduce_scatter x1, waiting for transfers between devices, body(): lax.psum_scatter(norm_terms, 'fsdp', scatter_dimension=0, tiled=True)  26.2 us
  transfers between devices with their start and end apart: 11, of which 8 were waited for; matrix products, arithmetic and copies ran while one was open for 6% of the time, Pallas kernels for 0%

commit v1 on v0

--- a/solution.py
+++ b/solution.py
@@ -3,6 +3,7 @@
 import jax.numpy as jnp
 from jax import lax
 from jax.sharding import PartitionSpec as P
+from jax.lax import psum
 
 KS = 7
 norm_eps = 1e-06
@@ -112,8 +113,8 @@
             )
     kernel_part = jnp.stack(kernel_rows).reshape(KS, KS, width)
     grad_x = (d_out.astype(jnp.float32) + back_conv).astype(jnp.bfloat16)
-    grad_kernel, grad_gain, grad_scale = lax.psum(
-        (kernel_part, gain_part, scale_part), ("dp", "fsdp", "rows")
+    grad_kernel, grad_gain, grad_scale = psum(
+        psum((kernel_part, gain_part, scale_part), ("fsdp", "rows")), "dp"
     )
     return (result, grad_x, grad_up, grad_down, grad_kernel, grad_gain, grad_scale)
 

time: 799 us -> 763 us (0.955)
  waiting for transfers between devices: 625 us -> 586 us
    reduce_scatter x1, waiting for transfers between devices: 201 us -> 161 us  [reduce_down(): lax.psum_scatter(down_part, ('dp', 'rows'), scatter_dimension=1, tiled=True)]
    psum x1 -> x2, blocking collectives: 42.3 us -> 44.7 us  [the longest x1 25.8 us: body(): psum((kernel_part, gain_part, scale_part), ('fsdp', 'rows'))]
    psum x1 -> x2, waiting for transfers between devices: 51.2 us -> 52.7 us  [the longest x1 52.7 us: body(): psum((kernel_part, gain_part, scale_part), ('fsdp', 'rows'))]
  transfers between devices with their start and end apart: 11 -> 12, of which waited for: 8 -> 8; matrix products, arithmetic and copies ran while one was open for 6% -> 7% of each run, Pallas kernels for 0% -> 0%
where the time goes in v1:
time: 763 us; the launch traced here: 762 us
  waiting for transfers between devices  586 us (77%)
  blocking collectives  65.2 us (9%)
  matrix products  44.7 us (6%)
  other arithmetic  30 us (4%)
  between operations  16 us (2%)
  local copies, waits for them, and re-layouts  12.1 us (2%)
  starting transfers between devices  7.97 us (1%)
    reduce_scatter x1, waiting for transfers between devices, body(): lax.psum_scatter(up_part, ('dp', 'rows'), scatter_dimension=0, tiled=True)  199 us
    reduce_scatter x1, waiting for transfers between devices, reduce_down(): lax.psum_scatter(down_part, ('dp', 'rows'), scatter_dimension=1, tiled=True)  161 us
    all_gather x1, waiting for transfers between devices, body(): down_full = lax.all_gather(w_down, ('dp', 'rows'), axis=1, tiled=True)  73.7 us
    all_gather x1, waiting for transfers between devices, body(): up_full = lax.all_gather(w_up, ('dp', 'rows'), axis=0, tiled=True)  55.8 us
    psum x1, waiting for transfers between devices, body(): psum((kernel_part, gain_part, scale_part), ('fsdp', 'rows'))  52.7 us
    reduce_scatter x1, waiting for transfers between devices, body(): lax.psum_scatter(norm_terms, 'fsdp', scatter_dimension=0, tiled=True)  26.2 us
    psum x1, blocking collectives, body(): psum((kernel_part, gain_part, scale_part), ('fsdp', 'rows'))  25.8 us
    psum x1, blocking collectives, body(): psum(psum((kernel_part, gain_part, scale_part), ('fsdp', 'rows')), 'dp')  18.9 us
  transfers between devices with their start and end apart: 12, of which 8 were waited for; matrix products, arithmetic and copies ran while one was open for 7% of the time, Pallas kernels for 0%

profile of v1, /device:TPU:0, one launch (start us, length us, event | category | flops | bytes accessed | tf_op | source)
XLA Modules:
  0.0 762.3 jit_solution(614729988281357002)
XLA Ops:
  9.8 2.4 collective-permute-start
  12.2 1.3 collective-permute-start.1
  13.5 1.3 slice_reduce_fusion.46
  16.4 1.4 collective-permute-done.1
  18.0 9.5 %fusion.103 = (f32[4,32]{1,0:T(4,128)S(1)}, f32[1,4,32,1536]{3,2,1,0:T(8,128)S(1)}) fusion(f32[1536]{0:T(1024)S(1)} %get-tuple-element.106, f32[1536]{0:T(1024)S(1)} %get-tuple-element.107, f32[1536]{0:T(1024)S(1)} %get-tuple-element.60, f32[1536]{0:T(1024)S(1)} %get-tuple-element.61, f32[1,10,32,1536]{3,2,1,0:T(8,128)S(1)} %maximum_convert_fusion, ...), kind=kLoop, calls=%fused_computation.314 | loop fusion | flops 19267456 | bytes 8641024 | tf_op jit(solution)/shard_map/reduce_sum | solution.py:56
  30.1 8.6 %all_gather.12 = bf16[256,1536]{1,0:T(8,128)(2,1)} all-gather(bf16[128,1536]{1,0:T(8,128)(2,1)S(1)} %multiply_convert_fusion.1), channel_id=1, replica_groups=mesh['dp'=4,'fsdp'=2,'rows'=4] {'fsdp'}, dimensions={0}, use_global_device_ids=true | all-gather | bytes 1179648 | tf_op jit(solution)/shard_map/all_gather | solution.py:62
  38.7 55.8 %all-gather.3.cloned.1.call-done = bf16[1536,3072]{1,0:T(8,128)(2,1)} async-done(((bf16[96,3072]{1,0:T(8,128)(2,1)}), bf16[1536,3072]{1,0:T(8,128)(2,1)}) %all-gather.3.cloned.1.call-update) | async-done | bytes 9437200 | tf_op jit(solution)/shard_map/all_gather | solution.py:63
  94.5 8.2 %fusion.106 = f32[256,3072]{1,0:T(8,128)} fusion(bf16[256,1536]{1,0:T(8,128)(2,1)} %all_gather.12, bf16[1536,3072]{1,0:T(8,128)(2,1)} %all-gather.3.cloned.1.call-done), kind=kOutput, calls=%fused_computation.317 | convolution fusion | flops 2415919104 | bytes 13369344 | tf_op jit(solution)/shard_map/dot_general | solution.py:65
  102.7 73.7 %all-gather.5.cloned.1.call-done = bf16[3072,1536]{0,1:T(8,128)(2,1)} async-done(((bf16[3072,96]{0,1:T(8,128)(2,1)}), bf16[3072,1536]{0,1:T(8,128)(2,1)}) %all-gather.5.cloned.1.call-update) | async-done | bytes 9437200 | tf_op jit(solution)/shard_map/all_gather | solution.py:64
  176.4 8.2 %convolution_convert_fusion = bf16[256,1536]{1,0:T(8,128)(2,1)} fusion(bf16[3072,1536]{0,1:T(8,128)(2,1)} %all-gather.5.cloned.1.call-done, f32[256,3072]{1,0:T(8,128)} %fusion.106), kind=kOutput, calls=%fused_computation.93 | convolution fusion | flops 2420244480 | bytes 13369344 | tf_op jit(solution)/shard_map/dot_general | solution.py:67
  184.6 15.7 %reduce-scatter.5.cloned.1.call-done = bf16[128,1536]{1,0:T(8,128)(2,1)} async-done(((bf16[256,1536]{1,0:T(8,128)(2,1)}), bf16[128,1536]{1,0:T(8,128)(2,1)}) %reduce-scatter.5.cloned.1.call-update) | async-done | bytes 393232 | tf_op jit(solution)/shard_map/reduce_scatter | solution.py:68
  200.3 2.7 fusion.7
  203.0 11.8 %all_gather.15 = bf16[256,1536]{1,0:T(8,128)(2,1)S(1)} all-gather(bf16[128,1536]{1,0:T(8,128)(2,1)S(1)} %get-tuple-element.116), channel_id=1, replica_groups=mesh['dp'=4,'fsdp'=2,'rows'=4] {'fsdp'}, dimensions={0}, use_global_device_ids=true | all-gather | bytes 1179648 | tf_op jit(solution)/shard_map/all_gather | solution.py:76
  215.7 5.5 fusion
  221.3 1.2 copy-done.7
  222.5 3.8 fusion.107
  226.4 26.2 %reduce-scatter.7.cloned.1.call-done = f32[128,1536]{1,0:T(8,128)} async-done(((f32[256,1536]{1,0:T(8,128)}), f32[128,1536]{1,0:T(8,128)}) %reduce-scatter.7.cloned.1.call-update) | async-done | bytes 786448 | tf_op jit(solution)/shard_map/reduce_scatter | solution.py:88
  252.6 2.0 multiply_reduce_fusion
  254.6 3.6 multiply_reduce_fusion.2
  258.2 1.2 multiply_reduce_fusion.3
  259.4 2.0 multiply_reduce_fusion.1
  263.5 52.7 %all-reduce.7.cloned.1.call-done = f32[7,7,1536]{2,1,0:T(8,128)} async-done(((f32[7,7,1536]{2,1,0:T(8,128)}), f32[7,7,1536]{2,1,0:T(8,128)}) %all-reduce.7.cloned.1.call-update) | async-done | bytes 301072 | tf_op jit(solution)/shard_map/psum | solution.py:117
  316.3 11.1 %fusion.102 = f32[3072,1536]{0,1:T(8,128)} fusion(bf16[256,1536]{1,0:T(8,128)(2,1)S(1)} %copy-done.3, f32[256,3072]{1,0:T(8,128)} %fusion.106), kind=kOutput, calls=%fused_computation.313 | convolution fusion | flops 2419851264 | bytes 22806528 | tf_op jit(solution)/shard_map/dot_general | solution.py:77
  329.0 7.9 %fusion.108 = f32[1536,3072]{1,0:T(8,128)} fusion(bf16[256,1536]{1,0:T(8,128)(2,1)S(1)} %copy-done.1, bf16[256,3072]{1,0:T(8,128)(2,1)S(1)} %copy-done.8), kind=kOutput, calls=%fused_computation.319 | convolution fusion | flops 2415919104 | bytes 21233664 | tf_op jit(solution)/shard_map/dot_general | solution.py:82
  337.5 2.5 collective-permute-start.2
  339.9 1.3 collective-permute-start.3
  341.3 25.8 %all-reduce.2 = (f32[1536]{0:T(1024)S(1)}, f32[1536]{0:T(1024)S(1)}) all-reduce(f32[1536]{0:T(1024)} %get-tuple-element.56, f32[1536]{0:T(1024)} %get-tuple-element.115), channel_id=1, replica_groups=mesh['dp'=4,'fsdp'=2,'rows'=4] {'fsdp','rows'}, use_global_device_ids=true, to_apply=%region_60.61 | all-reduce | flops 3072 | bytes 24576 | tf_op jit(solution)/shard_map/psum | solution.py:117
  367.1 18.9 %all-reduce.3 = (f32[1536]{0:T(1024)}, f32[1536]{0:T(1024)}) all-reduce(f32[1536]{0:T(1024)S(1)} %get-tuple-element.108, f32[1536]{0:T(1024)S(1)} %get-tuple-element.109), channel_id=1, replica_groups=mesh['dp'=4,'fsdp'=2,'rows'=4] {'dp'}, use_global_device_ids=true, to_apply=%region_61.62 | all-reduce | flops 3072 | bytes 24576 | tf_op jit(solution)/shard_map/psum | solution.py:116
  386.6 7.6 fusion.95
  394.2 160.8 %reduce-scatter.11.cloned.1.call-done = f32[3072,96]{0,1:T(8,128)} async-done(((f32[3072,1536]{0,1:T(8,128)}), f32[3072,96]{0,1:T(8,128)}) %reduce-scatter.11.cloned.1.call-update) | async-done | bytes 1179664 | tf_op jit(solution)/shard_map/reduce_scatter | solution.py:39
  555.0 198.8 %reduce-scatter.9.cloned.1.call-done = f32[96,3072]{1,0:T(8,128)} async-done(((f32[1536,3072]{1,0:T(8,128)}), f32[96,3072]{1,0:T(8,128)}) %reduce-scatter.9.cloned.1.call-update) | async-done | bytes 1179664 | tf_op jit(solution)/shard_map/reduce_scatter | solution.py:89
  753.7 1.7 copy.16
  (274 shorter events, 11.3 us)
Async XLA Ops:
  7.2 87.3 %all-gather.3.cloned.1.call-start = ((), (), s32[]{:S(2)}) async-start(), calls=%async_computation.4 | async-start | bytes 10027008 | tf_op jit(solution)/shard_map/all_gather | solution.py:63
  7.9 168.5 %all-gather.5.cloned.1.call-start = ((), (), s32[]{:S(2)}) async-start(), calls=%async_computation.5 | async-start | bytes 10027008 | tf_op jit(solution)/shard_map/all_gather | solution.py:64
  8.7 191.6 %reduce-scatter.5.cloned.1.call-start = ((), (), s32[]{:S(2)}) async-start(), calls=%async_computation.6 | async-start | bytes 1179648 | tf_op jit(solution)/shard_map/reduce_scatter | solution.py:68
  9.8 6.6 collective-permute-start
  12.2 5.6 collective-permute-start.1
  102.7 97.6 %copy-start.5 = (bf16[1,4,32,1536]{3,2,1,0:T(8,128)(2,1)S(1)}, bf16[1,4,32,1536]{3,2,1,0:T(8,128)(2,1)}, u32[]{:S(2)}) copy-start(bf16[1,4,32,1536]{3,2,1,0:T(8,128)(2,1)} %param.13) | copy-start | bytes 1179652
  184.6 68.0 %reduce-scatter.7.cloned.1.call-start = ((), (), s32[]{:S(2)}) async-start(), calls=%async_computation.7 | async-start | bytes 2359296 | tf_op jit(solution)/shard_map/reduce_scatter | solution.py:88
  226.3 89.9 %all-reduce.7.cloned.1.call-start = ((), (), s32[]{:S(2)}) async-start(), calls=%async_computation.10 | async-start | bytes 688128 | tf_op jit(solution)/shard_map/psum | solution.py:117
  259.4 56.9 %copy-start.3 = (bf16[256,1536]{1,0:T(8,128)(2,1)S(1)}, bf16[256,1536]{1,0:T(8,128)(2,1)}, u32[]{:S(2)}) copy-start(bf16[256,1536]{1,0:T(8,128)(2,1)} %copy-done.2) | copy-start | bytes 2359300
  263.4 130.7 %all-reduce.9.cloned.1.call-start = ((), (), s32[]{:S(2)}) async-start(), calls=%async_computation.11 | async-start | bytes 688128 | tf_op jit(solution)/shard_map/psum | solution.py:116
  316.3 238.7 %reduce-scatter.11.cloned.1.call-start = ((), (), s32[]{:S(2)}) async-start(), calls=%async_computation.9 | async-start | bytes 20054016 | tf_op jit(solution)/shard_map/reduce_scatter | solution.py:39
  327.4 426.3 %reduce-scatter.9.cloned.1.call-start = ((), (), s32[]{:S(2)}) async-start(), calls=%async_computation.8 | async-start | bytes 20054016 | tf_op jit(solution)/shard_map/reduce_scatter | solution.py:89
  337.0 49.2 %copy-start.6 = (bf16[1,4,32,1536]{3,2,1,0:T(8,128)(2,1)S(1)}, bf16[1,4,32,1536]{3,2,1,0:T(8,128)(2,1)}, u32[]{:S(2)}) copy-start(bf16[1,4,32,1536]{3,2,1,0:T(8,128)(2,1)} %param.13) | copy-start | bytes 1179652
  337.0 49.2 %copy-start.12 = (f32[1536]{0:T(1024)S(1)}, f32[1536]{0:T(1024)}, u32[]{:S(2)}) copy-start(f32[1536]{0:T(1024)} %copy-done.11) | copy-start | bytes 18436
  337.0 49.2 %copy-start.14 = (f32[1536]{0:T(1024)S(1)}, f32[1536]{0:T(1024)}, u32[]{:S(2)}) copy-start(f32[1536]{0:T(1024)} %copy-done.13) | copy-start | bytes 18436
  337.0 49.2 %copy-start.16 = (f32[1536]{0:T(1024)S(1)}, f32[1536]{0:T(1024)}, u32[]{:S(2)}) copy-start(f32[1536]{0:T(1024)} %copy-done.15) | copy-start | bytes 18436
  337.1 49.2 %copy-start.18 = (f32[1536]{0:T(1024)S(1)}, f32[1536]{0:T(1024)}, u32[]{:S(2)}) copy-start(f32[1536]{0:T(1024)} %copy-done.17) | copy-start | bytes 18436
  337.1 49.2 %copy-start.20 = (f32[1536]{0:T(1024)S(1)}, f32[1536]{0:T(1024)}, u32[]{:S(2)}) copy-start(f32[1536]{0:T(1024)} %copy-done.19) | copy-start | bytes 18436
  337.1 49.2 %copy-start.22 = (f32[1536]{0:T(1024)S(1)}, f32[1536]{0:T(1024)}, u32[]{:S(2)}) copy-start(f32[1536]{0:T(1024)} %copy-done.21) | copy-start | bytes 18436
  337.1 49.2 %copy-start.24 = (f32[1536]{0:T(1024)S(1)}, f32[1536]{0:T(1024)}, u32[]{:S(2)}) copy-start(f32[1536]{0:T(1024)} %copy-done.23) | copy-start | bytes 18436
  337.1 49.2 %copy-start.26 = (f32[1536]{0:T(1024)S(1)}, f32[1536]{0:T(1024)}, u32[]{:S(2)}) copy-start(f32[1536]{0:T(1024)} %copy-done.25) | copy-start | bytes 18436
  337.1 49.2 %copy-start.28 = (f32[1536]{0:T(1024)S(1)}, f32[1536]{0:T(1024)}, u32[]{:S(2)}) copy-start(f32[1536]{0:T(1024)} %copy-done.27) | copy-start | bytes 18436
  337.1 49.2 %copy-start.30 = (f32[1536]{0:T(1024)S(1)}, f32[1536]{0:T(1024)}, u32[]{:S(2)}) copy-start(f32[1536]{0:T(1024)} %copy-done.29) | copy-start | bytes 18436
  337.1 49.2 %copy-start.32 = (f32[1536]{0:T(1024)S(1)}, f32[1536]{0:T(1024)}, u32[]{:S(2)}) copy-start(f32[1536]{0:T(1024)} %copy-done.31) | copy-start | bytes 18436
  337.1 49.2 %copy-start.34 = (f32[1536]{0:T(1024)S(1)}, f32[1536]{0:T(1024)}, u32[]{:S(2)}) copy-start(f32[1536]{0:T(1024)} %copy-done.33) | copy-start | bytes 18436
  337.1 49.2 %copy-start.36 = (f32[1536]{0:T(1024)S(1)}, f32[1536]{0:T(1024)}, u32[]{:S(2)}) copy-start(f32[1536]{0:T(1024)} %copy-done.35) | copy-start | bytes 18436
  337.2 49.2 %copy-start.38 = (f32[1536]{0:T(1024)S(1)}, f32[1536]{0:T(1024)}, u32[]{:S(2)}) copy-start(f32[1536]{0:T(1024)} %copy-done.37) | copy-start | bytes 18436
  337.2 49.2 %copy-start.40 = (f32[1536]{0:T(1024)S(1)}, f32[1536]{0:T(1024)}, u32[]{:S(2)}) copy-start(f32[1536]{0:T(1024)} %copy-done.39) | copy-start | bytes 18436
  337.2 49.2 %copy-start.42 = (f32[1536]{0:T(1024)S(1)}, f32[1536]{0:T(1024)}, u32[]{:S(2)}) copy-start(f32[1536]{0:T(1024)} %copy-done.41) | copy-start | bytes 18436
  337.2 49.2 %copy-start.44 = (f32[1536]{0:T(1024)S(1)}, f32[1536]{0:T(1024)}, u32[]{:S(2)}) copy-start(f32[1536]{0:T(1024)} %copy-done.43) | copy-start | bytes 18436
  337.5 48.6 %collective-permute-start.2 = (bf16[1,3,32,1536]{3,2,1,0:T(8,128)(2,1)S(1)}, bf16[1,3,32,1536]{3,2,1,0:T(8,128)(2,1)S(1)}, u32[]{:S(2)}, u32[]{:S(2)}) collective-permute-start(bf16[1,3,32,1536]{3,2,1,0:T(8,128)(2,1)S(1)} %get-tuple-element.118), channel_id=1, source_target_pairs={{0,1},{1,2},{2,3},{4,5},{5,6},{6,7},{8,9},{9,10},{10,11},{12,13},{... | collective-permute-start | bytes 884744 | tf_op jit(solution)/shard_map/ppermute | solution.py:23
  339.9 46.1 %collective-permute-start.3 = (bf16[1,3,32,1536]{3,2,1,0:T(8,128)(2,1)S(1)}, bf16[1,3,32,1536]{3,2,1,0:T(8,128)(2,1)S(1)}, u32[]{:S(2)}, u32[]{:S(2)}) collective-permute-start(bf16[1,3,32,1536]{3,2,1,0:T(8,128)(2,1)S(1)} %get-tuple-element.119), channel_id=1, source_target_pairs={{1,0},{2,1},{3,2},{5,4},{6,5},{7,6},{9,8},{10,9},{11,10},{13,12},{... | collective-permute-start | bytes 884744 | tf_op jit(solution)/shard_map/ppermute | solution.py:24
  (74 other events, 1697.0 us)
Sparse Core Ops, SparseCore 0:
  10.3 84.1 all-gather.2
  96.8 79.5 all-gather.4
  184.7 15.5 reduce-scatter.4
  226.4 26.0 reduce-scatter.6
  263.6 52.6 all-reduce.6
  318.4 37.1 all-reduce.8
  360.3 194.6 reduce-scatter.10
  559.7 194.0 reduce-scatter.8
